TPU v7x, 512 devices: a whole 4x8x8 slice. The times are simulated.
512 devices in a mesh: clus: 256 (over z, y, x), samp: 2 (over core).
Axes of the slice: x: 4, y: 8, z: 8, core: 2. Of those that a mesh axis runs over, the one named last changes fastest.
Arguments:
- samples: float32 [262144, 256], P('clus', 'samp'), may hold values from -8 to 8
- sketch: float32 [256, 128], P('samp'), may hold values from -0.375 to 0.375
- leaf_slot: int32 [256, 4], P('clus'), may hold values from 0 to 3, each once within a row
Outputs:
- leaf_basis: float32 [262144, 128], P('clus')
- local_transfer: float32 [768, 256, 128], P('clus')
- top_transfer: float32 [256, 256, 128], P('clus')
- root_factor: float32 [128, 128], replicated
Inputs may be any that keep to these rules, and one draw needn't show every extreme that they name: Each row of leaf_slot names every number from 0 to 3 once.
All inputs are finite; a program needn't handle non-finite values.
Results may differ from a plain program's by a relative error of at most 0.0003.
Values sent between devices are 32-bit elements; how exact they have to be, the bound alone decides.
No kernel may reach another device: no remote copies, remote signals or barrier semaphores. Data moves between devices by JAX's collectives and lax.ppermute only.
A program may use at most 64 MiB of HBM per device.

v0:
```python
import jax
import jax.numpy as jnp
from jax import lax
from jax.sharding import PartitionSpec as P

NS_STEPS = 5
highest = lax.Precision.HIGHEST


def from_partner(block, axis, apart):
    count = lax.axis_size(axis)
    route = []
    for low in range(count):
        high = low | 1 << apart
        if high != low and high < count:
            route += [(low, high), (high, low)]
    return lax.ppermute(block, axis, route)


def factor(stacked):
    gram_matrix = jnp.einsum("mrk,mrl->mkl", stacked, stacked, precision=highest)
    width = gram_matrix.shape[1]
    identity = jnp.eye(width, dtype=jnp.float32)
    scale = jnp.einsum("mkk->m", gram_matrix)[:, None, None] + 1e-06
    start_root = gram_matrix / scale
    start_inverse = jnp.broadcast_to(identity, gram_matrix.shape)

    def newton_step(index, carry):
        root, inverse = carry
        middle = 1.5 * identity - 0.5 * jnp.einsum("mkl,mlj->mkj", inverse, root, precision=highest)
        return (
            jnp.einsum("mkl,mlj->mkj", root, middle, precision=highest),
            jnp.einsum("mkl,mlj->mkj", middle, inverse, precision=highest),
        )

    root, inverse = lax.fori_loop(0, NS_STEPS, newton_step, (start_root, start_inverse))
    scale_root = jnp.sqrt(scale)
    orthonormal = jnp.einsum("mrk,mkl->mrl", stacked, inverse, precision=highest) / scale_root
    return (orthonormal, root * scale_root)


def body(samples, sketch, leaf_slot):
    columns = sketch.shape[1]
    leaf_count = leaf_slot.shape[1]
    partial_value = jnp.dot(samples, sketch, precision=highest).reshape(leaf_count, -1, columns)
    sketched = lax.psum(partial_value, "samp")
    leaf_basis, triangle = factor(sketched)
    factors = triangle[leaf_slot[0]]
    local_list = []
    while factors.shape[0] > 1:
        stacked = factors.reshape(-1, 2 * columns, columns)
        transfer, factors = factor(stacked)
        local_list.append(transfer)
    local_transfer = jnp.concatenate(local_list, axis=0)
    position = lax.axis_index("clus")
    tree_depth = lax.axis_size("clus").bit_length() - 1
    top_out = jnp.zeros((1, 2 * columns, columns), jnp.float32)
    for level_bit in range(tree_depth):
        partner = from_partner(factors, "clus", level_bit)
        upper_half = position >> level_bit & 1 == 1
        stacked = jnp.where(
            upper_half,
            jnp.concatenate([partner, factors], axis=1),
            jnp.concatenate([factors, partner], axis=1),
        )
        transfer, factors = factor(stacked)
        owned = position % (2 << level_bit) == 1 << level_bit
        top_out = jnp.where(owned, transfer, top_out)
    return (leaf_basis.reshape(-1, columns), local_transfer, top_out, factors[0])


def solution(mesh):
    return jax.shard_map(
        body,
        mesh=mesh,
        in_specs=(P("clus", "samp"), P("samp", None), P("clus", None)),
        out_specs=(P("clus", None), P("clus", None, None), P("clus", None, None), P()),
        check_vma=False,
    )
```

profile of v0, /device:TPU:32, one launch (start us, length us, event | category | flops | bytes accessed | tf_op | source)
XLA Modules:
  0.0 200.3 jit_solution(17816542363103940892)
XLA Ops:
  7.2 1.0 copy-done
  8.2 2.2 %fusion.137 = f32[1024,128]{1,0:T(8,128)} fusion(f32[1024,128]{1,0:T(8,128)S(1)} %copy-done, f32[128,128]{1,0:T(8,128)} %param.26), kind=kOutput, calls=%fused_computation.230 | convolution fusion | flops 201326592 | bytes 1114112 | tf_op jit(solution)/shard_map/dot_general | solution.py:45
  11.8 39.1 %all-reduce.2.cloned.1.call-done = f32[4,256,128]{2,1,0:T(8,128)} async-done(((f32[4,256,128]{2,1,0:T(8,128)}), f32[4,256,128]{2,1,0:T(8,128)}) %all-reduce.2.cloned.1.call-update) | async-done | bytes 524304 | tf_op jit(solution)/shard_map/psum | solution.py:46
  50.9 2.3 %select_reduce_fusion = (f32[4]{0:T(128)S(1)}, f32[4,128,128]{2,1,0:T(8,128)S(1)}) fusion(pred[128,128]{1,0:T(8,128)(4,1)S(1)} %iota_compare_fusion.13, f32[4,256,128]{2,1,0:T(8,128)} %all-reduce.2.cloned.1.call-done), kind=kOutput, calls=%fused_computation.126 | convolution fusion | flops 201457664 | bytes 802832 | tf_op jit(solution)/shard_map/mrk,mrl->mkl/dot_general | solution.py:21
  53.5 8.8 %while.143 = (s32[]{:T(128)}, f32[4,128,128]{1,2,0:T(8,128)S(1)}, f32[4,128,128]{2,1,0:T(8,128)S(1)}, s32[]{:T(128)}) while((s32[]{:T(128)}, f32[4,128,128]{1,2,0:T(8,128)S(1)}, f32[4,128,128]{2,1,0:T(8,128)S(1)}, s32[]{:T(128)}) %tuple.231), condition=%wide.region_3.0_spmd.clone, body=%wide.region_2.0_spmd.clone.sunk | while | flops 302153728 | bytes 3538997 | solution.py:36
  64.1 5.6 %while.144 = (s32[]{:T(128)}, f32[2,128,128]{1,2,0:T(8,128)S(1)}, f32[2,128,128]{2,1,0:T(8,128)S(1)}, s32[]{:T(128)}) while((s32[]{:T(128)}, f32[2,128,128]{1,2,0:T(8,128)S(1)}, f32[2,128,128]{2,1,0:T(8,128)S(1)}, s32[]{:T(128)}) %tuple.234), condition=%wide.region_6.0_spmd.clone, body=%wide.region_5.0_spmd.clone.sunk | while | flops 151093248 | bytes 1835061 | solution.py:36
  69.9 1.0 select_reduce_fusion.10
  71.7 0.7 copy-done.3
  72.5 4.1 %while.145 = (s32[]{:T(128)}, f32[1,128,128]{1,2,0:T(8,128)S(1)}, f32[1,128,128]{2,1,0:T(8,128)S(1)}, s32[]{:T(128)}) while((s32[]{:T(128)}, f32[1,128,128]{1,2,0:T(8,128)S(1)}, f32[1,128,128]{2,1,0:T(8,128)S(1)}, s32[]{:T(128)}) %tuple.267), condition=%wide.region_9.0_spmd.clone, body=%wide.region_8.0_spmd.clone.sunk | while | flops 75563008 | bytes 852021 | solution.py:36
  76.9 3.4 %collective-permute-start = (f32[1,128,128]{1,2,0:T(8,128)S(1)}, f32[1,128,128]{1,2,0:T(8,128)S(1)}, u32[]{:S(2)}, u32[]{:S(2)}) collective-permute-start(f32[1,128,128]{1,2,0:T(8,128)S(1)} %broadcast_multiply_fusion.9), channel_id=1, source_target_pairs={{0,2},{2,0},{4,6},{6,4},{8,10},{10,8},{12,14},{14,12},{16,18},{18,... | collective-permute-start | bytes 196616 | tf_op jit(solution)/shard_map/ppermute | solution.py:17
  80.6 1.4 convolution_divide_fusion
  82.0 0.8 pad_maximum_fusion
  83.1 0.9 select_reduce_fusion.9
  84.8 0.7 copy-done.4
  85.6 4.1 %while.146 = (s32[]{:T(128)}, f32[1,128,128]{1,2,0:T(8,128)S(1)}, f32[1,128,128]{2,1,0:T(8,128)S(1)}, s32[]{:T(128)}) while((s32[]{:T(128)}, f32[1,128,128]{1,2,0:T(8,128)S(1)}, f32[1,128,128]{2,1,0:T(8,128)S(1)}, s32[]{:T(128)}) %tuple.268), condition=%wide.region_12.13_spmd.clone, body=%wide.region_11.12_spmd.clone.sunk | while | flops 75563008 | bytes 852021 | solution.py:36
  89.6 4.9 %collective-permute-start.1 = (f32[1,128,128]{1,2,0:T(8,128)S(1)}, f32[1,128,128]{1,2,0:T(8,128)S(1)}, u32[]{:S(2)}, u32[]{:S(2)}) collective-permute-start(f32[1,128,128]{1,2,0:T(8,128)S(1)} %broadcast_multiply_fusion.8), channel_id=1, source_target_pairs={{0,4},{4,0},{2,6},{6,2},{8,12},{12,8},{10,14},{14,10},{16,20},{20,... | collective-permute-start | bytes 196616 | tf_op jit(solution)/shard_map/ppermute | solution.py:17
  95.0 2.4 %collective-permute-done.1 = f32[1,128,128]{1,2,0:T(8,128)S(1)} collective-permute-done((f32[1,128,128]{1,2,0:T(8,128)S(1)}, f32[1,128,128]{1,2,0:T(8,128)S(1)}, u32[]{:S(2)}, u32[]{:S(2)}) %collective-permute-start.1) | collective-permute-done | bytes 65568 | tf_op jit(solution)/shard_map/ppermute | solution.py:17
  97.3 0.9 select_reduce_fusion.8
  99.0 0.7 copy-done.5
  99.7 4.1 %while.147 = (s32[]{:T(128)}, f32[1,128,128]{1,2,0:T(8,128)S(1)}, f32[1,128,128]{2,1,0:T(8,128)S(1)}, s32[]{:T(128)}) while((s32[]{:T(128)}, f32[1,128,128]{1,2,0:T(8,128)S(1)}, f32[1,128,128]{2,1,0:T(8,128)S(1)}, s32[]{:T(128)}) %tuple.269), condition=%wide.region_15.16_spmd.clone, body=%wide.region_14.15_spmd.clone.sunk | while | flops 75563008 | bytes 852021 | solution.py:36
  103.8 2.5 %collective-permute-start.2 = (f32[1,128,128]{1,2,0:T(8,128)S(1)}, f32[1,128,128]{1,2,0:T(8,128)S(1)}, u32[]{:S(2)}, u32[]{:S(2)}) collective-permute-start(f32[1,128,128]{1,2,0:T(8,128)S(1)} %broadcast_multiply_fusion.7), channel_id=1, source_target_pairs={{0,8},{8,0},{2,10},{10,2},{4,12},{12,4},{6,14},{14,6},{16,24},{24,... | collective-permute-start | bytes 196616 | tf_op jit(solution)/shard_map/ppermute | solution.py:17
  106.7 3.2 %collective-permute-done.2 = f32[1,128,128]{1,2,0:T(8,128)S(1)} collective-permute-done((f32[1,128,128]{1,2,0:T(8,128)S(1)}, f32[1,128,128]{1,2,0:T(8,128)S(1)}, u32[]{:S(2)}, u32[]{:S(2)}) %collective-permute-start.2) | collective-permute-done | bytes 65568 | tf_op jit(solution)/shard_map/ppermute | solution.py:17
  110.0 0.9 select_reduce_fusion.7
  111.7 0.7 copy-done.6
  112.4 4.1 %while.148 = (s32[]{:T(128)}, f32[1,128,128]{1,2,0:T(8,128)S(1)}, f32[1,128,128]{2,1,0:T(8,128)S(1)}, s32[]{:T(128)}) while((s32[]{:T(128)}, f32[1,128,128]{1,2,0:T(8,128)S(1)}, f32[1,128,128]{2,1,0:T(8,128)S(1)}, s32[]{:T(128)}) %tuple.270), condition=%wide.region_18.19_spmd.clone, body=%wide.region_17.18_spmd.clone.sunk | while | flops 75563008 | bytes 852021 | solution.py:36
  116.5 2.5 %collective-permute-start.3 = (f32[1,128,128]{1,2,0:T(8,128)S(1)}, f32[1,128,128]{1,2,0:T(8,128)S(1)}, u32[]{:S(2)}, u32[]{:S(2)}) collective-permute-start(f32[1,128,128]{1,2,0:T(8,128)S(1)} %broadcast_multiply_fusion.6), channel_id=1, source_target_pairs={{0,16},{16,0},{2,18},{18,2},{4,20},{20,4},{6,22},{22,6},{8,24},{24... | collective-permute-start | bytes 196616 | tf_op jit(solution)/shard_map/ppermute | solution.py:17
  119.4 4.8 %collective-permute-done.3 = f32[1,128,128]{1,2,0:T(8,128)S(1)} collective-permute-done((f32[1,128,128]{1,2,0:T(8,128)S(1)}, f32[1,128,128]{1,2,0:T(8,128)S(1)}, u32[]{:S(2)}, u32[]{:S(2)}) %collective-permute-start.3) | collective-permute-done | bytes 65568 | tf_op jit(solution)/shard_map/ppermute | solution.py:17
  124.3 0.9 select_reduce_fusion.6
  126.0 0.7 copy-done.7
  126.7 4.1 %while.149 = (s32[]{:T(128)}, f32[1,128,128]{1,2,0:T(8,128)S(1)}, f32[1,128,128]{2,1,0:T(8,128)S(1)}, s32[]{:T(128)}) while((s32[]{:T(128)}, f32[1,128,128]{1,2,0:T(8,128)S(1)}, f32[1,128,128]{2,1,0:T(8,128)S(1)}, s32[]{:T(128)}) %tuple.271), condition=%wide.region_21.22_spmd.clone, body=%wide.region_20.21_spmd.clone.sunk | while | flops 75563008 | bytes 852021 | solution.py:36
  130.8 3.5 %collective-permute-start.4 = (f32[1,128,128]{1,2,0:T(8,128)S(1)}, f32[1,128,128]{1,2,0:T(8,128)S(1)}, u32[]{:S(2)}, u32[]{:S(2)}) collective-permute-start(f32[1,128,128]{1,2,0:T(8,128)S(1)} %broadcast_multiply_fusion.5), channel_id=1, source_target_pairs={{0,32},{32,0},{2,34},{34,2},{4,36},{36,4},{6,38},{38,6},{8,40},{40... | collective-permute-start | bytes 196616 | tf_op jit(solution)/shard_map/ppermute | solution.py:17
  134.7 6.2 %collective-permute-done.4 = f32[1,128,128]{1,2,0:T(8,128)S(1)} collective-permute-done((f32[1,128,128]{1,2,0:T(8,128)S(1)}, f32[1,128,128]{1,2,0:T(8,128)S(1)}, u32[]{:S(2)}, u32[]{:S(2)}) %collective-permute-start.4) | collective-permute-done | bytes 65568 | tf_op jit(solution)/shard_map/ppermute | solution.py:17
  140.9 0.9 select_reduce_fusion.5
  142.6 0.7 copy-done.8
  143.3 4.1 %while.150 = (s32[]{:T(128)}, f32[1,128,128]{1,2,0:T(8,128)S(1)}, f32[1,128,128]{2,1,0:T(8,128)S(1)}, s32[]{:T(128)}) while((s32[]{:T(128)}, f32[1,128,128]{1,2,0:T(8,128)S(1)}, f32[1,128,128]{2,1,0:T(8,128)S(1)}, s32[]{:T(128)}) %tuple.272), condition=%wide.region_24.25_spmd.clone, body=%wide.region_23.24_spmd.clone.sunk | while | flops 75563008 | bytes 852021 | solution.py:36
  147.4 4.0 %collective-permute-start.5 = (f32[1,128,128]{1,2,0:T(8,128)S(1)}, f32[1,128,128]{1,2,0:T(8,128)S(1)}, u32[]{:S(2)}, u32[]{:S(2)}) collective-permute-start(f32[1,128,128]{1,2,0:T(8,128)S(1)} %broadcast_multiply_fusion.4), channel_id=1, source_target_pairs={{0,64},{64,0},{2,66},{66,2},{4,68},{68,4},{6,70},{70,6},{8,72},{72... | collective-permute-start | bytes 196616 | tf_op jit(solution)/shard_map/ppermute | solution.py:17
  151.8 1.8 collective-permute-done.5
  153.6 0.9 select_reduce_fusion.4
  156.1 4.1 %while.151 = (s32[]{:T(128)}, f32[1,128,128]{1,2,0:T(8,128)S(1)}, f32[1,128,128]{2,1,0:T(8,128)S(1)}, s32[]{:T(128)}) while((s32[]{:T(128)}, f32[1,128,128]{1,2,0:T(8,128)S(1)}, f32[1,128,128]{2,1,0:T(8,128)S(1)}, s32[]{:T(128)}) %tuple.273), condition=%wide.region_27.28_spmd.clone, body=%wide.region_26.27_spmd.clone.sunk | while | flops 75563008 | bytes 852021 | solution.py:36
  160.2 5.0 %collective-permute-start.6 = (f32[1,128,128]{1,2,0:T(8,128)S(1)}, f32[1,128,128]{1,2,0:T(8,128)S(1)}, u32[]{:S(2)}, u32[]{:S(2)}) collective-permute-start(f32[1,128,128]{1,2,0:T(8,128)S(1)} %broadcast_multiply_fusion.3), channel_id=1, source_target_pairs={{0,128},{128,0},{2,130},{130,2},{4,132},{132,4},{6,134},{134,6},{8... | collective-permute-start | bytes 196616 | tf_op jit(solution)/shard_map/ppermute | solution.py:17
  165.6 1.8 collective-permute-done.6
  167.4 0.9 select_reduce_fusion.3
  169.8 4.1 %while.152 = (s32[]{:T(128)}, f32[1,128,128]{1,2,0:T(8,128)S(1)}, f32[1,128,128]{2,1,0:T(8,128)S(1)}, s32[]{:T(128)}) while((s32[]{:T(128)}, f32[1,128,128]{1,2,0:T(8,128)S(1)}, f32[1,128,128]{2,1,0:T(8,128)S(1)}, s32[]{:T(128)}) %tuple.274), condition=%wide.region_30.31_spmd.clone, body=%wide.region_29.30_spmd.clone.sunk | while | flops 75563008 | bytes 852021 | solution.py:36
  173.9 8.9 %collective-permute-start.7 = (f32[1,128,128]{1,2,0:T(8,128)S(1)}, f32[1,128,128]{1,2,0:T(8,128)S(1)}, u32[]{:S(2)}, u32[]{:S(2)}) collective-permute-start(f32[1,128,128]{1,2,0:T(8,128)S(1)} %broadcast_multiply_fusion.2), channel_id=1, source_target_pairs={{0,256},{256,0},{2,258},{258,2},{4,260},{260,4},{6,262},{262,6},{8... | collective-permute-start | bytes 196616 | tf_op jit(solution)/shard_map/ppermute | solution.py:17
  183.2 1.9 collective-permute-done.7
  185.2 0.9 select_reduce_fusion.2
  187.6 4.1 %while.153 = (s32[]{:T(128)}, f32[1,128,128]{1,2,0:T(8,128)S(1)}, f32[1,128,128]{2,1,0:T(8,128)S(1)}, s32[]{:T(128)}) while((s32[]{:T(128)}, f32[1,128,128]{1,2,0:T(8,128)S(1)}, f32[1,128,128]{2,1,0:T(8,128)S(1)}, s32[]{:T(128)}) %tuple.266), condition=%wide.region_33.34_spmd.clone, body=%wide.region_32.33_spmd.clone.sunk | while | flops 75563008 | bytes 852021 | solution.py:36
  192.4 1.0 fusion.73
  (371 shorter events, 59.7 us)
Async XLA Ops:
  7.2 1.0 copy-start
  7.2 43.8 %all-reduce.2.cloned.1.call-start = ((), (), s32[]{:S(2)}) async-start(), calls=%async_computation | async-start | bytes 1048576 | tf_op jit(solution)/shard_map/psum | solution.py:46
  10.5 0.6 copy-start.1
  11.1 0.7 copy-start.12
  71.6 0.8 copy-start.3
  76.6 4.0 %copy-start.11 = (f32[4,256,128]{2,1,0:T(8,128)S(1)}, f32[4,256,128]{2,1,0:T(8,128)}, u32[]{:S(2)}) copy-start(f32[4,256,128]{2,1,0:T(8,128)} %all-reduce.2.cloned.1.call-done) | copy-start | bytes 1572868
  76.9 6.2 %collective-permute-start = (f32[1,128,128]{1,2,0:T(8,128)S(1)}, f32[1,128,128]{1,2,0:T(8,128)S(1)}, u32[]{:S(2)}, u32[]{:S(2)}) collective-permute-start(f32[1,128,128]{1,2,0:T(8,128)S(1)} %broadcast_multiply_fusion.9), channel_id=1, source_target_pairs={{0,2},{2,0},{4,6},{6,4},{8,10},{10,8},{12,14},{14,12},{16,18},{18,... | collective-permute-start | bytes 196616 | tf_op jit(solution)/shard_map/ppermute | solution.py:17
  84.7 0.8 copy-start.4
  89.6 7.7 %collective-permute-start.1 = (f32[1,128,128]{1,2,0:T(8,128)S(1)}, f32[1,128,128]{1,2,0:T(8,128)S(1)}, u32[]{:S(2)}, u32[]{:S(2)}) collective-permute-start(f32[1,128,128]{1,2,0:T(8,128)S(1)} %broadcast_multiply_fusion.8), channel_id=1, source_target_pairs={{0,4},{4,0},{2,6},{6,2},{8,12},{12,8},{10,14},{14,10},{16,20},{20,... | collective-permute-start | bytes 196616 | tf_op jit(solution)/shard_map/ppermute | solution.py:17
  98.9 0.8 copy-start.5
  103.8 6.2 %collective-permute-start.2 = (f32[1,128,128]{1,2,0:T(8,128)S(1)}, f32[1,128,128]{1,2,0:T(8,128)S(1)}, u32[]{:S(2)}, u32[]{:S(2)}) collective-permute-start(f32[1,128,128]{1,2,0:T(8,128)S(1)} %broadcast_multiply_fusion.7), channel_id=1, source_target_pairs={{0,8},{8,0},{2,10},{10,2},{4,12},{12,4},{6,14},{14,6},{16,24},{24,... | collective-permute-start | bytes 196616 | tf_op jit(solution)/shard_map/ppermute | solution.py:17
  111.6 0.8 copy-start.6
  116.5 7.8 %collective-permute-start.3 = (f32[1,128,128]{1,2,0:T(8,128)S(1)}, f32[1,128,128]{1,2,0:T(8,128)S(1)}, u32[]{:S(2)}, u32[]{:S(2)}) collective-permute-start(f32[1,128,128]{1,2,0:T(8,128)S(1)} %broadcast_multiply_fusion.6), channel_id=1, source_target_pairs={{0,16},{16,0},{2,18},{18,2},{4,20},{20,4},{6,22},{22,6},{8,24},{24... | collective-permute-start | bytes 196616 | tf_op jit(solution)/shard_map/ppermute | solution.py:17
  125.9 0.8 copy-start.7
  130.8 10.1 %collective-permute-start.4 = (f32[1,128,128]{1,2,0:T(8,128)S(1)}, f32[1,128,128]{1,2,0:T(8,128)S(1)}, u32[]{:S(2)}, u32[]{:S(2)}) collective-permute-start(f32[1,128,128]{1,2,0:T(8,128)S(1)} %broadcast_multiply_fusion.5), channel_id=1, source_target_pairs={{0,32},{32,0},{2,34},{34,2},{4,36},{36,4},{6,38},{38,6},{8,40},{40... | collective-permute-start | bytes 196616 | tf_op jit(solution)/shard_map/ppermute | solution.py:17
  142.5 0.8 copy-start.8
  147.4 6.2 %collective-permute-start.5 = (f32[1,128,128]{1,2,0:T(8,128)S(1)}, f32[1,128,128]{1,2,0:T(8,128)S(1)}, u32[]{:S(2)}, u32[]{:S(2)}) collective-permute-start(f32[1,128,128]{1,2,0:T(8,128)S(1)} %broadcast_multiply_fusion.4), channel_id=1, source_target_pairs={{0,64},{64,0},{2,66},{66,2},{4,68},{68,4},{6,70},{70,6},{8,72},{72... | collective-permute-start | bytes 196616 | tf_op jit(solution)/shard_map/ppermute | solution.py:17
  155.2 0.8 copy-start.9
  160.2 7.2 %collective-permute-start.6 = (f32[1,128,128]{1,2,0:T(8,128)S(1)}, f32[1,128,128]{1,2,0:T(8,128)S(1)}, u32[]{:S(2)}, u32[]{:S(2)}) collective-permute-start(f32[1,128,128]{1,2,0:T(8,128)S(1)} %broadcast_multiply_fusion.3), channel_id=1, source_target_pairs={{0,128},{128,0},{2,130},{130,2},{4,132},{132,4},{6,134},{134,6},{8... | collective-permute-start | bytes 196616 | tf_op jit(solution)/shard_map/ppermute | solution.py:17
  169.0 0.8 copy-start.10
  173.9 11.2 %collective-permute-start.7 = (f32[1,128,128]{1,2,0:T(8,128)S(1)}, f32[1,128,128]{1,2,0:T(8,128)S(1)}, u32[]{:S(2)}, u32[]{:S(2)}) collective-permute-start(f32[1,128,128]{1,2,0:T(8,128)S(1)} %broadcast_multiply_fusion.2), channel_id=1, source_target_pairs={{0,256},{256,0},{2,258},{258,2},{4,260},{260,4},{6,262},{262,6},{8... | collective-permute-start | bytes 196616 | tf_op jit(solution)/shard_map/ppermute | solution.py:17
  186.7 0.8 copy-start.2
Sparse Core Ops, SparseCore 0:
  11.5 39.4 all-reduce.1
where the time goes:
time: 201 us; the launch traced here: 200 us
  matrix products  66.6 us (33%)
  waiting for transfers between devices  61.6 us (31%)
  starting transfers between devices  34.7 us (17%)
  between operations  21 us (10%)
  local copies, waits for them, and re-layouts  11.7 us (6%)
  loops' own time  2.47 us (1%)
  other arithmetic  2.16 us (1%)
    psum x1, waiting for transfers between devices, body(): sketched = lax.psum(partial_value, 'samp')  39.1 us
    ppermute x8, starting transfers between devices, from_partner(): return lax.ppermute(block, axis, route)  34.7 us
    ppermute x8, waiting for transfers between devices, from_partner(): return lax.ppermute(block, axis, route)  22.5 us
    dot_general x55, matrix products, newton_step(): jnp.einsum('mkl,mlj->mkj', root, middle, precision=highest)  17.8 us
    dot_general x55, matrix products, newton_step(): jnp.einsum('mkl,mlj->mkj', inverse, root, precision=highest)  17.3 us
    dot_general x55, matrix products, newton_step(): jnp.einsum('mkl,mlj->mkj', middle, inverse, precision=highest)  12.4 us
    dot_general x11, matrix products, factor(): jnp.einsum('mrk,mrl->mkl', stacked, stacked, precision=highest)  11 us
    unnamed x37, local copies, waits for them, and re-layouts  9.91 us
  transfers between devices with their start and end apart: 9, of which 9 were waited for; matrix products, arithmetic and copies ran while one was open for 3% of the time, Pallas kernels for 0%

commit v1 on v0

--- a/solution.py
+++ b/solution.py
@@ -2,6 +2,7 @@
 import jax.numpy as jnp
 from jax import lax
 from jax.sharding import PartitionSpec as P
+from jax.lax import all_gather
 
 NS_STEPS = 5
 highest = lax.Precision.HIGHEST
@@ -43,7 +44,7 @@
     columns = sketch.shape[1]
     leaf_count = leaf_slot.shape[1]
     partial_value = jnp.dot(samples, sketch, precision=highest).reshape(leaf_count, -1, columns)
-    sketched = lax.psum(partial_value, "samp")
+    sketched = all_gather(partial_value, axis_name="samp").sum(axis=0)
     leaf_basis, triangle = factor(sketched)
     factors = triangle[leaf_slot[0]]
     local_list = []

time: 201 us -> 184 us (0.915)
  waiting for transfers between devices: 61.6 us -> 44.3 us
    psum x1 -> x0, waiting for transfers between devices: 39.1 us -> none  [body(): sketched = lax.psum(partial_value, 'samp')]
    all_gather x0 -> x1, waiting for transfers between devices: none -> 20.4 us  [body(): sketched = all_gather(partial_value, axis_name='samp').sum(axis=0)]
    unnamed x37 -> x35, local copies, waits for them, and re-layouts: 9.91 us -> 9.91 us
  transfers between devices with their start and end apart: 9 -> 9, of which waited for: 9 -> 9; matrix products, arithmetic and copies ran while one was open for 3% -> 2% of each run, Pallas kernels for 0% -> 0%
where the time goes in v1:
time: 184 us; the launch traced here: 183 us
  matrix products  65.4 us (36%)
  waiting for transfers between devices  44.3 us (24%)
  starting transfers between devices  34.7 us (19%)
  between operations  21 us (11%)
  local copies, waits for them, and re-layouts  11.7 us (6%)
  other arithmetic  3.51 us (2%)
  loops' own time  2.47 us (1%)
    ppermute x8, starting transfers between devices, from_partner(): return lax.ppermute(block, axis, route)  34.7 us
    ppermute x8, waiting for transfers between devices, from_partner(): return lax.ppermute(block, axis, route)  23.9 us
    all_gather x1, waiting for transfers between devices, body(): sketched = all_gather(partial_value, axis_name='samp').sum(axis=0)  20.4 us
    dot_general x55, matrix products, newton_step(): jnp.einsum('mkl,mlj->mkj', root, middle, precision=highest)  17.8 us
    dot_general x55, matrix products, newton_step(): jnp.einsum('mkl,mlj->mkj', inverse, root, precision=highest)  17.3 us
    dot_general x55, matrix products, newton_step(): jnp.einsum('mkl,mlj->mkj', middle, inverse, precision=highest)  12.4 us
    unnamed x35, local copies, waits for them, and re-layouts  9.91 us
    dot_general x11, matrix products, factor(): jnp.einsum('mrk,mrl->mkl', stacked, stacked, precision=highest)  9.8 us
  transfers between devices with their start and end apart: 9, of which 9 were waited for; matrix products, arithmetic and copies ran while one was open for 2% of the time, Pallas kernels for 0%

profile of v1, /device:TPU:32, one launch (start us, length us, event | category | flops | bytes accessed | tf_op | source)
XLA Modules:
  0.0 183.1 jit_solution(2888992823658169233)
XLA Ops:
  7.2 1.0 copy-done
  8.2 2.2 %fusion.137 = f32[1024,128]{1,0:T(8,128)} fusion(f32[1024,128]{1,0:T(8,128)S(1)} %copy-done, f32[128,128]{1,0:T(8,128)} %param.26), kind=kOutput, calls=%fused_computation.230 | convolution fusion | flops 201326592 | bytes 1114112 | tf_op jit(solution)/shard_map/dot_general | solution.py:46
  11.8 20.4 %all-gather.2.cloned.1.call-done = f32[2,4,256,128]{3,2,1,0:T(8,128)} async-done(((f32[1,4,256,128]{3,2,1,0:T(8,128)}), f32[2,4,256,128]{3,2,1,0:T(8,128)}) %all-gather.2.cloned.1.call-update) | async-done | bytes 1048592 | tf_op jit(solution)/shard_map/all_gather | solution.py:47
  32.2 1.3 reduce_sum.108
  33.5 1.1 select_reduce_fusion
  34.9 8.8 %while.143 = (s32[]{:T(128)}, f32[4,128,128]{1,2,0:T(8,128)S(1)}, f32[4,128,128]{2,1,0:T(8,128)S(1)}, s32[]{:T(128)}) while((s32[]{:T(128)}, f32[4,128,128]{1,2,0:T(8,128)S(1)}, f32[4,128,128]{2,1,0:T(8,128)S(1)}, s32[]{:T(128)}) %tuple.242), condition=%wide.region_3.0_spmd.clone, body=%wide.region_2.0_spmd.clone.sunk | while | flops 302153728 | bytes 3538997 | solution.py:37
  45.5 5.6 %while.144 = (s32[]{:T(128)}, f32[2,128,128]{1,2,0:T(8,128)S(1)}, f32[2,128,128]{2,1,0:T(8,128)S(1)}, s32[]{:T(128)}) while((s32[]{:T(128)}, f32[2,128,128]{1,2,0:T(8,128)S(1)}, f32[2,128,128]{2,1,0:T(8,128)S(1)}, s32[]{:T(128)}) %tuple.245), condition=%wide.region_6.0_spmd.clone, body=%wide.region_5.0_spmd.clone.sunk | while | flops 151093248 | bytes 1835061 | solution.py:37
  51.3 1.0 select_reduce_fusion.10
  53.1 0.7 copy-done.3
  53.8 4.1 %while.145 = (s32[]{:T(128)}, f32[1,128,128]{1,2,0:T(8,128)S(1)}, f32[1,128,128]{2,1,0:T(8,128)S(1)}, s32[]{:T(128)}) while((s32[]{:T(128)}, f32[1,128,128]{1,2,0:T(8,128)S(1)}, f32[1,128,128]{2,1,0:T(8,128)S(1)}, s32[]{:T(128)}) %tuple.278), condition=%wide.region_9.0_spmd.clone, body=%wide.region_8.0_spmd.clone.sunk | while | flops 75563008 | bytes 852021 | solution.py:37
  57.9 1.4 convolution_divide_fusion
  59.7 3.4 %collective-permute-start = (f32[1,128,128]{1,2,0:T(8,128)S(1)}, f32[1,128,128]{1,2,0:T(8,128)S(1)}, u32[]{:S(2)}, u32[]{:S(2)}) collective-permute-start(f32[1,128,128]{1,2,0:T(8,128)S(1)} %broadcast_multiply_fusion.9), channel_id=1, source_target_pairs={{0,2},{2,0},{4,6},{6,4},{8,10},{10,8},{12,14},{14,12},{16,18},{18,... | collective-permute-start | bytes 196616 | tf_op jit(solution)/shard_map/ppermute | solution.py:18
  63.4 0.8 pad_maximum_fusion
  64.1 1.8 collective-permute-done
  65.9 0.9 select_reduce_fusion.9
  68.3 4.1 %while.146 = (s32[]{:T(128)}, f32[1,128,128]{1,2,0:T(8,128)S(1)}, f32[1,128,128]{2,1,0:T(8,128)S(1)}, s32[]{:T(128)}) while((s32[]{:T(128)}, f32[1,128,128]{1,2,0:T(8,128)S(1)}, f32[1,128,128]{2,1,0:T(8,128)S(1)}, s32[]{:T(128)}) %tuple.279), condition=%wide.region_12.13_spmd.clone, body=%wide.region_11.12_spmd.clone.sunk | while | flops 75563008 | bytes 852021 | solution.py:37
  72.4 4.9 %collective-permute-start.1 = (f32[1,128,128]{1,2,0:T(8,128)S(1)}, f32[1,128,128]{1,2,0:T(8,128)S(1)}, u32[]{:S(2)}, u32[]{:S(2)}) collective-permute-start(f32[1,128,128]{1,2,0:T(8,128)S(1)} %broadcast_multiply_fusion.8), channel_id=1, source_target_pairs={{0,4},{4,0},{2,6},{6,2},{8,12},{12,8},{10,14},{14,10},{16,20},{20,... | collective-permute-start | bytes 196616 | tf_op jit(solution)/shard_map/ppermute | solution.py:18
  77.7 2.4 %collective-permute-done.1 = f32[1,128,128]{1,2,0:T(8,128)S(1)} collective-permute-done((f32[1,128,128]{1,2,0:T(8,128)S(1)}, f32[1,128,128]{1,2,0:T(8,128)S(1)}, u32[]{:S(2)}, u32[]{:S(2)}) %collective-permute-start.1) | collective-permute-done | bytes 65568 | tf_op jit(solution)/shard_map/ppermute | solution.py:18
  80.1 0.9 select_reduce_fusion.8
  81.8 0.7 copy-done.5
  82.5 4.1 %while.147 = (s32[]{:T(128)}, f32[1,128,128]{1,2,0:T(8,128)S(1)}, f32[1,128,128]{2,1,0:T(8,128)S(1)}, s32[]{:T(128)}) while((s32[]{:T(128)}, f32[1,128,128]{1,2,0:T(8,128)S(1)}, f32[1,128,128]{2,1,0:T(8,128)S(1)}, s32[]{:T(128)}) %tuple.280), condition=%wide.region_15.16_spmd.clone, body=%wide.region_14.15_spmd.clone.sunk | while | flops 75563008 | bytes 852021 | solution.py:37
  86.6 2.5 %collective-permute-start.2 = (f32[1,128,128]{1,2,0:T(8,128)S(1)}, f32[1,128,128]{1,2,0:T(8,128)S(1)}, u32[]{:S(2)}, u32[]{:S(2)}) collective-permute-start(f32[1,128,128]{1,2,0:T(8,128)S(1)} %broadcast_multiply_fusion.7), channel_id=1, source_target_pairs={{0,8},{8,0},{2,10},{10,2},{4,12},{12,4},{6,14},{14,6},{16,24},{24,... | collective-permute-start | bytes 196616 | tf_op jit(solution)/shard_map/ppermute | solution.py:18
  89.5 3.2 %collective-permute-done.2 = f32[1,128,128]{1,2,0:T(8,128)S(1)} collective-permute-done((f32[1,128,128]{1,2,0:T(8,128)S(1)}, f32[1,128,128]{1,2,0:T(8,128)S(1)}, u32[]{:S(2)}, u32[]{:S(2)}) %collective-permute-start.2) | collective-permute-done | bytes 65568 | tf_op jit(solution)/shard_map/ppermute | solution.py:18
  92.8 0.9 select_reduce_fusion.7
  94.5 0.7 copy-done.6
  95.2 4.1 %while.148 = (s32[]{:T(128)}, f32[1,128,128]{1,2,0:T(8,128)S(1)}, f32[1,128,128]{2,1,0:T(8,128)S(1)}, s32[]{:T(128)}) while((s32[]{:T(128)}, f32[1,128,128]{1,2,0:T(8,128)S(1)}, f32[1,128,128]{2,1,0:T(8,128)S(1)}, s32[]{:T(128)}) %tuple.281), condition=%wide.region_18.19_spmd.clone, body=%wide.region_17.18_spmd.clone.sunk | while | flops 75563008 | bytes 852021 | solution.py:37
  99.3 2.5 %collective-permute-start.3 = (f32[1,128,128]{1,2,0:T(8,128)S(1)}, f32[1,128,128]{1,2,0:T(8,128)S(1)}, u32[]{:S(2)}, u32[]{:S(2)}) collective-permute-start(f32[1,128,128]{1,2,0:T(8,128)S(1)} %broadcast_multiply_fusion.6), channel_id=1, source_target_pairs={{0,16},{16,0},{2,18},{18,2},{4,20},{20,4},{6,22},{22,6},{8,24},{24... | collective-permute-start | bytes 196616 | tf_op jit(solution)/shard_map/ppermute | solution.py:18
  102.2 4.8 %collective-permute-done.3 = f32[1,128,128]{1,2,0:T(8,128)S(1)} collective-permute-done((f32[1,128,128]{1,2,0:T(8,128)S(1)}, f32[1,128,128]{1,2,0:T(8,128)S(1)}, u32[]{:S(2)}, u32[]{:S(2)}) %collective-permute-start.3) | collective-permute-done | bytes 65568 | tf_op jit(solution)/shard_map/ppermute | solution.py:18
  107.0 0.9 select_reduce_fusion.6
  108.7 0.7 copy-done.7
  109.5 4.1 %while.149 = (s32[]{:T(128)}, f32[1,128,128]{1,2,0:T(8,128)S(1)}, f32[1,128,128]{2,1,0:T(8,128)S(1)}, s32[]{:T(128)}) while((s32[]{:T(128)}, f32[1,128,128]{1,2,0:T(8,128)S(1)}, f32[1,128,128]{2,1,0:T(8,128)S(1)}, s32[]{:T(128)}) %tuple.282), condition=%wide.region_21.22_spmd.clone, body=%wide.region_20.21_spmd.clone.sunk | while | flops 75563008 | bytes 852021 | solution.py:37
  113.6 3.5 %collective-permute-start.4 = (f32[1,128,128]{1,2,0:T(8,128)S(1)}, f32[1,128,128]{1,2,0:T(8,128)S(1)}, u32[]{:S(2)}, u32[]{:S(2)}) collective-permute-start(f32[1,128,128]{1,2,0:T(8,128)S(1)} %broadcast_multiply_fusion.5), channel_id=1, source_target_pairs={{0,32},{32,0},{2,34},{34,2},{4,36},{36,4},{6,38},{38,6},{8,40},{40... | collective-permute-start | bytes 196616 | tf_op jit(solution)/shard_map/ppermute | solution.py:18
  117.5 6.2 %collective-permute-done.4 = f32[1,128,128]{1,2,0:T(8,128)S(1)} collective-permute-done((f32[1,128,128]{1,2,0:T(8,128)S(1)}, f32[1,128,128]{1,2,0:T(8,128)S(1)}, u32[]{:S(2)}, u32[]{:S(2)}) %collective-permute-start.4) | collective-permute-done | bytes 65568 | tf_op jit(solution)/shard_map/ppermute | solution.py:18
  123.7 0.9 select_reduce_fusion.5
  126.1 4.1 %while.150 = (s32[]{:T(128)}, f32[1,128,128]{1,2,0:T(8,128)S(1)}, f32[1,128,128]{2,1,0:T(8,128)S(1)}, s32[]{:T(128)}) while((s32[]{:T(128)}, f32[1,128,128]{1,2,0:T(8,128)S(1)}, f32[1,128,128]{2,1,0:T(8,128)S(1)}, s32[]{:T(128)}) %tuple.283), condition=%wide.region_24.25_spmd.clone, body=%wide.region_23.24_spmd.clone.sunk | while | flops 75563008 | bytes 852021 | solution.py:37
  130.2 4.0 %collective-permute-start.5 = (f32[1,128,128]{1,2,0:T(8,128)S(1)}, f32[1,128,128]{1,2,0:T(8,128)S(1)}, u32[]{:S(2)}, u32[]{:S(2)}) collective-permute-start(f32[1,128,128]{1,2,0:T(8,128)S(1)} %broadcast_multiply_fusion.4), channel_id=1, source_target_pairs={{0,64},{64,0},{2,66},{66,2},{4,68},{68,4},{6,70},{70,6},{8,72},{72... | collective-permute-start | bytes 196616 | tf_op jit(solution)/shard_map/ppermute | solution.py:18
  134.6 1.8 collective-permute-done.5
  136.4 0.9 select_reduce_fusion.4
  138.9 4.1 %while.151 = (s32[]{:T(128)}, f32[1,128,128]{1,2,0:T(8,128)S(1)}, f32[1,128,128]{2,1,0:T(8,128)S(1)}, s32[]{:T(128)}) while((s32[]{:T(128)}, f32[1,128,128]{1,2,0:T(8,128)S(1)}, f32[1,128,128]{2,1,0:T(8,128)S(1)}, s32[]{:T(128)}) %tuple.284), condition=%wide.region_27.28_spmd.clone, body=%wide.region_26.27_spmd.clone.sunk | while | flops 75563008 | bytes 852021 | solution.py:37
  142.9 5.0 %collective-permute-start.6 = (f32[1,128,128]{1,2,0:T(8,128)S(1)}, f32[1,128,128]{1,2,0:T(8,128)S(1)}, u32[]{:S(2)}, u32[]{:S(2)}) collective-permute-start(f32[1,128,128]{1,2,0:T(8,128)S(1)} %broadcast_multiply_fusion.3), channel_id=1, source_target_pairs={{0,128},{128,0},{2,130},{130,2},{4,132},{132,4},{6,134},{134,6},{8... | collective-permute-start | bytes 196616 | tf_op jit(solution)/shard_map/ppermute | solution.py:18
  148.4 1.8 collective-permute-done.6
  150.2 0.9 select_reduce_fusion.3
  152.6 4.1 %while.152 = (s32[]{:T(128)}, f32[1,128,128]{1,2,0:T(8,128)S(1)}, f32[1,128,128]{2,1,0:T(8,128)S(1)}, s32[]{:T(128)}) while((s32[]{:T(128)}, f32[1,128,128]{1,2,0:T(8,128)S(1)}, f32[1,128,128]{2,1,0:T(8,128)S(1)}, s32[]{:T(128)}) %tuple.285), condition=%wide.region_30.31_spmd.clone, body=%wide.region_29.30_spmd.clone.sunk | while | flops 75563008 | bytes 852021 | solution.py:37
  156.7 8.9 %collective-permute-start.7 = (f32[1,128,128]{1,2,0:T(8,128)S(1)}, f32[1,128,128]{1,2,0:T(8,128)S(1)}, u32[]{:S(2)}, u32[]{:S(2)}) collective-permute-start(f32[1,128,128]{1,2,0:T(8,128)S(1)} %broadcast_multiply_fusion.2), channel_id=1, source_target_pairs={{0,256},{256,0},{2,258},{258,2},{4,260},{260,4},{6,262},{262,6},{8... | collective-permute-start | bytes 196616 | tf_op jit(solution)/shard_map/ppermute | solution.py:18
  166.0 1.9 %collective-permute-done.7 = f32[1,128,128]{1,2,0:T(8,128)S(1)} collective-permute-done((f32[1,128,128]{1,2,0:T(8,128)S(1)}, f32[1,128,128]{1,2,0:T(8,128)S(1)}, u32[]{:S(2)}, u32[]{:S(2)}) %collective-permute-start.7) | collective-permute-done | bytes 65568 | tf_op jit(solution)/shard_map/ppermute | solution.py:18
  167.9 0.9 select_reduce_fusion.2
  170.4 4.1 %while.153 = (s32[]{:T(128)}, f32[1,128,128]{1,2,0:T(8,128)S(1)}, f32[1,128,128]{2,1,0:T(8,128)S(1)}, s32[]{:T(128)}) while((s32[]{:T(128)}, f32[1,128,128]{1,2,0:T(8,128)S(1)}, f32[1,128,128]{2,1,0:T(8,128)S(1)}, s32[]{:T(128)}) %tuple.277), condition=%wide.region_33.34_spmd.clone, body=%wide.region_32.33_spmd.clone.sunk | while | flops 75563008 | bytes 852021 | solution.py:37
  175.2 1.0 fusion.73
  (370 shorter events, 60.8 us)
Async XLA Ops:
  7.2 1.0 copy-start
  7.2 25.0 %all-gather.2.cloned.1.call-start = ((), (), s32[]{:S(2)}) async-start(), calls=%async_computation | async-start | bytes 1572864 | tf_op jit(solution)/shard_map/all_gather | solution.py:47
  10.5 0.6 copy-start.1
  11.1 0.7 copy-start.11
  53.0 0.8 copy-start.3
  59.7 6.2 %collective-permute-start = (f32[1,128,128]{1,2,0:T(8,128)S(1)}, f32[1,128,128]{1,2,0:T(8,128)S(1)}, u32[]{:S(2)}, u32[]{:S(2)}) collective-permute-start(f32[1,128,128]{1,2,0:T(8,128)S(1)} %broadcast_multiply_fusion.9), channel_id=1, source_target_pairs={{0,2},{2,0},{4,6},{6,4},{8,10},{10,8},{12,14},{14,12},{16,18},{18,... | collective-permute-start | bytes 196616 | tf_op jit(solution)/shard_map/ppermute | solution.py:18
  67.5 0.8 copy-start.4
  72.4 7.7 %collective-permute-start.1 = (f32[1,128,128]{1,2,0:T(8,128)S(1)}, f32[1,128,128]{1,2,0:T(8,128)S(1)}, u32[]{:S(2)}, u32[]{:S(2)}) collective-permute-start(f32[1,128,128]{1,2,0:T(8,128)S(1)} %broadcast_multiply_fusion.8), channel_id=1, source_target_pairs={{0,4},{4,0},{2,6},{6,2},{8,12},{12,8},{10,14},{14,10},{16,20},{20,... | collective-permute-start | bytes 196616 | tf_op jit(solution)/shard_map/ppermute | solution.py:18
  81.7 0.8 copy-start.5
  86.6 6.2 %collective-permute-start.2 = (f32[1,128,128]{1,2,0:T(8,128)S(1)}, f32[1,128,128]{1,2,0:T(8,128)S(1)}, u32[]{:S(2)}, u32[]{:S(2)}) collective-permute-start(f32[1,128,128]{1,2,0:T(8,128)S(1)} %broadcast_multiply_fusion.7), channel_id=1, source_target_pairs={{0,8},{8,0},{2,10},{10,2},{4,12},{12,4},{6,14},{14,6},{16,24},{24,... | collective-permute-start | bytes 196616 | tf_op jit(solution)/shard_map/ppermute | solution.py:18
  94.4 0.8 copy-start.6
  99.3 7.8 %collective-permute-start.3 = (f32[1,128,128]{1,2,0:T(8,128)S(1)}, f32[1,128,128]{1,2,0:T(8,128)S(1)}, u32[]{:S(2)}, u32[]{:S(2)}) collective-permute-start(f32[1,128,128]{1,2,0:T(8,128)S(1)} %broadcast_multiply_fusion.6), channel_id=1, source_target_pairs={{0,16},{16,0},{2,18},{18,2},{4,20},{20,4},{6,22},{22,6},{8,24},{24... | collective-permute-start | bytes 196616 | tf_op jit(solution)/shard_map/ppermute | solution.py:18
  108.6 0.8 copy-start.7
  113.6 10.1 %collective-permute-start.4 = (f32[1,128,128]{1,2,0:T(8,128)S(1)}, f32[1,128,128]{1,2,0:T(8,128)S(1)}, u32[]{:S(2)}, u32[]{:S(2)}) collective-permute-start(f32[1,128,128]{1,2,0:T(8,128)S(1)} %broadcast_multiply_fusion.5), channel_id=1, source_target_pairs={{0,32},{32,0},{2,34},{34,2},{4,36},{36,4},{6,38},{38,6},{8,40},{40... | collective-permute-start | bytes 196616 | tf_op jit(solution)/shard_map/ppermute | solution.py:18
  125.3 0.8 copy-start.8
  130.2 6.2 %collective-permute-start.5 = (f32[1,128,128]{1,2,0:T(8,128)S(1)}, f32[1,128,128]{1,2,0:T(8,128)S(1)}, u32[]{:S(2)}, u32[]{:S(2)}) collective-permute-start(f32[1,128,128]{1,2,0:T(8,128)S(1)} %broadcast_multiply_fusion.4), channel_id=1, source_target_pairs={{0,64},{64,0},{2,66},{66,2},{4,68},{68,4},{6,70},{70,6},{8,72},{72... | collective-permute-start | bytes 196616 | tf_op jit(solution)/shard_map/ppermute | solution.py:18
  138.0 0.8 copy-start.9
  142.9 7.2 %collective-permute-start.6 = (f32[1,128,128]{1,2,0:T(8,128)S(1)}, f32[1,128,128]{1,2,0:T(8,128)S(1)}, u32[]{:S(2)}, u32[]{:S(2)}) collective-permute-start(f32[1,128,128]{1,2,0:T(8,128)S(1)} %broadcast_multiply_fusion.3), channel_id=1, source_target_pairs={{0,128},{128,0},{2,130},{130,2},{4,132},{132,4},{6,134},{134,6},{8... | collective-permute-start | bytes 196616 | tf_op jit(solution)/shard_map/ppermute | solution.py:18
  151.8 0.8 copy-start.10
  156.7 11.2 %collective-permute-start.7 = (f32[1,128,128]{1,2,0:T(8,128)S(1)}, f32[1,128,128]{1,2,0:T(8,128)S(1)}, u32[]{:S(2)}, u32[]{:S(2)}) collective-permute-start(f32[1,128,128]{1,2,0:T(8,128)S(1)} %broadcast_multiply_fusion.2), channel_id=1, source_target_pairs={{0,256},{256,0},{2,258},{258,2},{4,260},{260,4},{6,262},{262,6},{8... | collective-permute-start | bytes 196616 | tf_op jit(solution)/shard_map/ppermute | solution.py:18
  169.5 0.8 copy-start.2
Sparse Core Ops, SparseCore 0:
  10.7 21.4 all-gather.1
